TPU v7x, 512 devices: a whole 4x4x16 slice. The times are simulated.
512 devices in a mesh: ctx: 32 (over z_hi, x, y), exp: 16 (over z_lo, core).
Axes of the slice: x: 4, y: 4, z: 16 (z_hi: 2, z_lo: 8; z = z_hi * 8 + z_lo), core: 2. Of those that a mesh axis runs over, the one named last changes fastest.
Arguments:
- residual: bfloat16 [4096, 4096], P(('ctx', 'exp')), may hold values from -6 to 6
- queries: bfloat16 [4096, 4096], P('ctx', 'exp'), may hold values from -8 to 8
- keys: bfloat16 [4096, 256], P('ctx'), may hold values from -8 to 8
- values: bfloat16 [4096, 256], P('ctx'), may hold values from -6 to 6
- span_pos: int32 [64], replicated, may hold values from 0 to 63, each once
- out_proj: bfloat16 [4096, 4096], P('exp'), may hold values from -0.71875 to 0.71875
- norm_gain: float32 [4096], replicated, may hold values from 0.25 to 1.75
- expert_gate: bfloat16 [16, 4096, 768], P('exp', None, 'ctx'), may hold values from -0.09375 to 0.09375
- expert_up: bfloat16 [16, 4096, 768], P('exp', None, 'ctx'), may hold values from -0.09375 to 0.09375
- expert_ids: int32 [4096, 8], P(('ctx', 'exp')), may hold values from 0 to 15, all different within a row; in each aligned block of 8 rows (0 to 7, 8 to 15, ...) at most 6 rows name the same one
- route_weight: float32 [4096, 8], P(('ctx', 'exp')), may hold values from 0.25 to 2
Outputs:
- mixed: bfloat16 [4096, 4096], P(('ctx', 'exp'))
- routed: bfloat16 [4096, 8, 768], P(('ctx', 'exp'))
Inputs may be any that keep to these rules, and one draw needn't show every extreme that they name: `span_pos`: every span number appears once. `expert_ids`: each row names 8 different experts; among the rows of one device (8 rows in a row, aligned) no expert is named more than 6 times, and in some device's rows some expert is named exactly 6 times.
All inputs are finite; a program needn't handle non-finite values.
Results may differ from a plain program's by a relative error of at most 0.035.
Values may be sent and summed in bfloat16 or wider, within the bound.
No kernel may reach another device: no remote copies, remote signals or barrier semaphores. Data moves between devices by JAX's collectives and lax.ppermute only.
A program may use at most 128 MiB of HBM per device.

v0:
```python
import math
import jax
import jax.numpy as jnp
import numpy as np
from jax import lax
from jax.sharding import Mesh
from jax.sharding import PartitionSpec as P

D = 4096
HQ = 32
KVH = 2
HD = 128
FE = 768
EXPERTS = 16
TOPK = 8
CH = 64
CTX = ("zh", "x", "y")
EXP = ("zl", "c")


def stored_positions(span_pos, rows):
    span = rows // CH
    table = span[:, None] == jnp.arange(span_pos.shape[0], dtype=jnp.int32)[None, :]
    base = jnp.sum(jnp.where(table, span_pos[None, :], 0), axis=1)
    return base * CH + rows % CH


def doubling_bits(n):
    bits = []
    b = n // 2
    while b >= 1:
        bits.append(b)
        b //= 2
    return bits


def gather_by_doubling(piece, n):
    idx = lax.axis_index(CTX)
    cur = piece
    order = [0]
    for bit in doubling_bits(n):
        other = lax.ppermute(cur, CTX, [(i, i ^ bit) for i in range(n)])
        low = idx & bit == 0
        cur = jnp.where(low, jnp.concatenate([cur, other]), jnp.concatenate([other, cur]))
        order = order + [o + bit for o in order]
    return (cur, order)


def shards(
    residual,
    queries,
    keys,
    values,
    span_pos,
    out_proj,
    norm_gain,
    expert_gate,
    expert_up,
    expert_ids,
    route_weight,
    n_ctx,
    n_xy,
    n_zh,
):
    tok_rows = queries.shape[0]
    per_device = queries.shape[1] // HD
    group = HQ // KVH
    ctx_index = lax.axis_index(CTX)
    exp_index = lax.axis_index(EXP)
    n_exp = EXPERTS
    fe_dev = expert_gate.shape[2]
    w_local = jnp.concatenate([expert_gate[0].T, expert_up[0].T], axis=0)
    w_all = lax.all_gather(w_local, "zh", axis=0, tiled=True)
    w_all = lax.all_gather(w_all, ("x", "y"), axis=0, tiled=True)
    kv_head = exp_index * per_device // group
    own_keys = lax.dynamic_slice_in_dim(keys, kv_head * HD, HD, 1)
    own_values = lax.dynamic_slice_in_dim(values, kv_head * HD, HD, 1)
    kv_local = jnp.concatenate([own_keys, own_values], axis=1)
    kv_all, order = gather_by_doubling(kv_local, n_ctx)
    key_piece = kv_all[:, :HD]
    value_piece = kv_all[:, HD:]
    length = key_piece.shape[0]
    block_ctx = jnp.asarray(np.array(order, np.int32))
    key_rows_all = jnp.repeat(block_ctx, tok_rows) * tok_rows + jnp.tile(
        jnp.arange(tok_rows, dtype=jnp.int32), n_ctx
    )
    query_pos = stored_positions(
        span_pos, ctx_index * tok_rows + jnp.arange(tok_rows, dtype=jnp.int32)
    )
    query_heads = queries.reshape(tok_rows, per_device, HD)
    scale = 1.0 / math.sqrt(HD)
    carry = (
        jnp.full((per_device, tok_rows), -1e30, jnp.float32),
        jnp.zeros((per_device, tok_rows), jnp.float32),
        jnp.zeros((per_device, tok_rows, HD), jnp.float32),
    )
    block = min(length, 1024)
    for begin in range(0, length, block):
        stop = min(begin + block, length)
        attend_key_piece = key_piece[begin:stop]
        attend_value_piece = value_piece[begin:stop]
        attend_running, attend_total, attend_accum = carry
        key_pos = stored_positions(span_pos, key_rows_all[begin:stop])
        scores = (
            jnp.einsum(
                "tqd,nd->qtn", query_heads, attend_key_piece, preferred_element_type=jnp.float32
            )
            * scale
        )
        visible = key_pos[None, None, :] <= query_pos[None, :, None]
        block_top = jnp.max(jnp.where(visible, scores, -1e30), axis=2)
        new_top = jnp.maximum(attend_running, block_top)
        factor = jnp.exp(attend_running - new_top)
        probs = jnp.where(visible, jnp.exp(scores - new_top[:, :, None]), 0.0)
        attend_total = attend_total * factor + jnp.sum(probs, axis=2)
        summed = jnp.einsum(
            "qtn,nd->qtd",
            probs.astype(jnp.bfloat16),
            attend_value_piece,
            preferred_element_type=jnp.float32,
        )
        attend_accum = attend_accum * factor[:, :, None] + summed
        carry = (new_top, attend_total, attend_accum)
    running, total, accum = carry
    attn = (accum / total[:, :, None]).astype(jnp.bfloat16)
    attn = jnp.transpose(attn, (1, 0, 2)).reshape(tok_rows, per_device * HD)
    tok_dev = residual.shape[0]
    share = jnp.dot(attn, out_proj, preferred_element_type=jnp.float32).astype(jnp.bfloat16)
    shares = lax.all_to_all(
        share.reshape(n_exp, tok_dev, D), EXP, split_axis=0, concat_axis=0, tiled=True
    )
    head_total = jnp.sum(shares.astype(jnp.float32), axis=0)
    mixed = (residual.astype(jnp.float32) + head_total).astype(jnp.bfloat16)
    mixed_f = mixed.astype(jnp.float32)
    square = jnp.mean(mixed_f * mixed_f, axis=1, keepdims=True)
    normed = (mixed_f * lax.rsqrt(square + 1e-06) * norm_gain[None, :]).astype(jnp.bfloat16)
    most_slots = 3 * tok_dev // 4
    ids_flat = expert_ids.reshape(-1)
    onehot = (ids_flat[:, None] == jnp.arange(EXPERTS, dtype=jnp.int32)[None, :]).astype(jnp.int32)
    earlier = jnp.cumsum(onehot, axis=0) - onehot
    slot = jnp.sum(earlier * onehot, axis=1)
    target = ids_flat * most_slots + slot
    placing = (
        target[:, None] == jnp.arange(EXPERTS * most_slots, dtype=jnp.int32)[None, :]
    ).astype(jnp.bfloat16)
    placing = jnp.sum(placing.reshape(tok_dev, TOPK, EXPERTS * most_slots), axis=1)
    outgoing = jnp.einsum("ts,td->sd", placing, normed, preferred_element_type=jnp.float32).astype(
        jnp.bfloat16
    )
    outgoing = outgoing.reshape(EXPERTS, most_slots, D)
    received = lax.all_to_all(outgoing, EXP, split_axis=0, concat_axis=0, tiled=True)
    received = received.reshape(EXPERTS * most_slots, D)
    proj = jnp.einsum("sd,fd->sf", received, w_all, preferred_element_type=jnp.float32)
    proj = proj.reshape(EXPERTS * most_slots, n_xy, n_zh, 2, fe_dev)
    hidden = jax.nn.silu(proj[:, :, :, 0]) * proj[:, :, :, 1]
    hidden = jnp.transpose(hidden, (0, 2, 1, 3)).reshape(EXPERTS, most_slots, FE)
    returned = (
        lax.all_to_all(hidden.astype(jnp.bfloat16), EXP, split_axis=0, concat_axis=0, tiled=True)
        .astype(jnp.float32)
        .reshape(EXPERTS * most_slots, FE)
    )
    picked = jnp.take(returned, target, axis=0)
    routed = (picked * route_weight.reshape(-1)[:, None]).astype(jnp.bfloat16)
    return (mixed, routed.reshape(tok_dev, TOPK, FE))


def solution(mesh):
    n_ctx = mesh.shape["ctx"]
    n_exp = mesh.shape["exp"]
    n_zh = 2
    n_xy = n_ctx // n_zh
    side = int(round(math.sqrt(n_xy)))
    n_zl = n_exp // 2
    fine = Mesh(mesh.devices.reshape(n_zh, side, n_xy // side, n_zl, 2), CTX + EXP)
    tok = CTX + EXP
    in_specs = (
        P(tok, None),
        P(CTX, EXP),
        P(CTX, None),
        P(CTX, None),
        P(),
        P(EXP, None),
        P(),
        P(EXP, None, CTX),
        P(EXP, None, CTX),
        P(tok, None),
        P(tok, None),
    )
    out_specs = (P(tok, None), P(tok, None, None))

    def body(*args):
        return shards(*args, n_ctx=n_ctx, n_xy=n_xy, n_zh=n_zh)

    return jax.shard_map(body, mesh=fine, in_specs=in_specs, out_specs=out_specs, check_vma=False)
```

profile of v0, /device:TPU:269, one launch (start us, length us, event | category | flops | bytes accessed | tf_op | source)
XLA Modules:
  0.0 315.9 jit_solution(2825617987332319186)
XLA Ops:
  7.2 0.0 copy-start
  7.2 0.0 copy-start.5
  7.2 0.0 all-gather.2.cloned.1.call-start
  7.2 1.2 pad_maximum_fusion
  8.4 0.0 copy-start.8
  8.5 0.0 copy-start.9
  8.5 23.8 %all_gather.6 = bf16[96,4096]{1,0:T(8,128)(2,1)} all-gather(bf16[48,4096]{1,0:T(8,128)(2,1)S(1)} %pad_maximum_fusion), channel_id=1, replica_groups=mesh['zh'=2,'x'=4,'y'=4,'zl'=8,'c'=2] {'zh'}, dimensions={0}, use_global_device_ids=true | all-gather | bytes 1179648 | tf_op jit(solution)/shard_map/all_gather | solution.py:73
  32.3 0.0 all-gather.2.cloned.1.call-update
  32.4 2.1 collective-permute-start
  34.5 19.4 %collective-permute-done = bf16[128,256]{1,0:T(8,128)(2,1)S(1)} collective-permute-done((bf16[128,256]{1,0:T(8,128)(2,1)S(1)}, bf16[128,256]{1,0:T(8,128)(2,1)S(1)}, u32[]{:S(2)}, u32[]{:S(2)}) %collective-permute-start) | collective-permute-done | bytes 65568 | tf_op jit(solution)/shard_map/ppermute | solution.py:42
  54.0 2.1 collective-permute-start.1
  56.1 5.6 %collective-permute-done.1 = bf16[256,256]{1,0:T(8,128)(2,1)S(1)} collective-permute-done((bf16[256,256]{1,0:T(8,128)(2,1)S(1)}, bf16[256,256]{1,0:T(8,128)(2,1)S(1)}, u32[]{:S(2)}, u32[]{:S(2)}) %collective-permute-start.1) | collective-permute-done | bytes 131104 | tf_op jit(solution)/shard_map/ppermute | solution.py:42
  61.8 0.1 maximum_select_fusion.3
  61.9 2.8 collective-permute-start.2
  64.7 5.3 %collective-permute-done.2 = bf16[512,256]{1,0:T(8,128)(2,1)S(1)} collective-permute-done((bf16[512,256]{1,0:T(8,128)(2,1)S(1)}, bf16[512,256]{1,0:T(8,128)(2,1)S(1)}, u32[]{:S(2)}, u32[]{:S(2)}) %collective-permute-start.2) | collective-permute-done | bytes 262176 | tf_op jit(solution)/shard_map/ppermute | solution.py:42
  70.1 0.2 maximum_select_fusion.2
  70.3 3.9 %collective-permute-start.3 = (bf16[1024,256]{1,0:T(8,128)(2,1)S(1)}, bf16[1024,256]{1,0:T(8,128)(2,1)S(1)}, u32[]{:S(2)}, u32[]{:S(2)}) collective-permute-start(bf16[1024,256]{1,0:T(8,128)(2,1)S(1)} %maximum_select_fusion.2), channel_id=1, source_target_pairs={{0,32},{16,48},{32,0},{48,16},{64,96},{80,112},{96,64},{112,80},{1... | collective-permute-start | bytes 1572872 | tf_op jit(solution)/shard_map/ppermute | solution.py:42
  74.3 0.1 select_reduce_fusion.9
  74.4 0.1 iota_add_fusion
  74.4 21.2 %collective-permute-done.3 = bf16[1024,256]{1,0:T(8,128)(2,1)S(1)} collective-permute-done((bf16[1024,256]{1,0:T(8,128)(2,1)S(1)}, bf16[1024,256]{1,0:T(8,128)(2,1)S(1)}, u32[]{:S(2)}, u32[]{:S(2)}) %collective-permute-start.3) | collective-permute-done | bytes 524320 | tf_op jit(solution)/shard_map/ppermute | solution.py:42
  95.6 0.2 maximum_select_fusion.1
  95.8 3.1 collective-permute-start.4
  99.0 0.2 select_reduce_fusion.4
  99.3 0.8 broadcast_compare_fusion.1
  100.1 0.0 copy-start.10
  100.1 19.2 %collective-permute-done.4 = bf16[2048,256]{1,0:T(8,128)(2,1)S(1)} collective-permute-done((bf16[2048,256]{1,0:T(8,128)(2,1)S(1)}, bf16[2048,256]{1,0:T(8,128)(2,1)S(1)}, u32[]{:S(2)}, u32[]{:S(2)}) %collective-permute-start.4) | collective-permute-done | bytes 1048608 | tf_op jit(solution)/shard_map/ppermute | solution.py:42
  119.3 0.5 maximum_select_fusion
  119.8 0.3 select_reduce_fusion
  120.2 0.3 select_reduce_fusion.1
  120.5 0.3 select_reduce_fusion.2
  120.9 0.3 select_reduce_fusion.3
  121.2 0.4 fusion.14
  121.7 0.4 fusion.18
  122.1 0.4 fusion.12
  122.5 0.4 fusion.10
  122.9 0.4 fusion.8
  123.2 0.4 fusion.13
  123.6 0.0 copy-start.3
  123.6 1.5 fusion
  125.1 42.7 %all-to-all-start = ((bf16[16,8,4096]{2,1,0:T(8,128)(2,1)}), bf16[16,8,4096]{2,1,0:T(8,128)(2,1)S(1)}, u32[]{:S(2)}, u32[]{:S(2)}) async-start(bf16[16,8,4096]{2,1,0:T(8,128)(2,1)} %fusion), calls=%async_computation | async-start | bytes 2097152 | tf_op jit(solution)/shard_map/all_to_all | solution.py:129
  167.9 0.1 reshape.360
  167.9 0.1 fusion.59
  168.0 0.1 reduce_window_sum.11
  168.1 0.2 select_reduce_fusion.8
  168.3 0.1 reduce_sum.147
  168.4 0.1 fusion.61
  168.5 43.8 %all-to-all-done = bf16[16,8,4096]{2,1,0:T(8,128)(2,1)S(1)} async-done(((bf16[16,8,4096]{2,1,0:T(8,128)(2,1)}), bf16[16,8,4096]{2,1,0:T(8,128)(2,1)S(1)}, u32[]{:S(2)}, u32[]{:S(2)}) %all-to-all-start) | async-done | bytes 1048608 | tf_op jit(solution)/shard_map/all_to_all | solution.py:129
  212.3 0.1 convert_reduce_fusion
  212.4 0.1 fusion.45
  212.6 1.3 convolution_convert_fusion.1
  213.9 1.4 reshape.361
  215.3 60.6 %all_to_all.15 = bf16[16,6,4096]{2,1,0:T(8,128)(2,1)} all-to-all(bf16[16,6,4096]{2,1,0:T(8,128)(2,1)S(1)} %reshape.361), channel_id=1, replica_groups=mesh['zh'=2,'x'=4,'y'=4,'zl'=8,'c'=2] {'zl','c'}, dimensions={0} | all-to-all | bytes 1572864 | tf_op jit(solution)/shard_map/all_to_all | solution.py:151
  276.0 1.4 reshape.383
  277.4 0.0 all-gather.2.cloned.1.call-done
  277.4 6.4 %fusion.22 = f32[96,16,2,2,24]{0,4,3,2,1:T(8,128)S(1)} fusion(bf16[16,2,2,24,4096]{4,3,2,1,0:T(8,128)(2,1)} %bitcast.294, bf16[96,4096,1,1,1]{1,0,2,3,4:T(8,128)(2,1)S(1)} %reshape.383), kind=kOutput, calls=%fused_computation.44 | convolution fusion | flops 1207959552 | bytes 13959168 | tf_op jit(solution)/shard_map/sd,fd->sf/dot_general | solution.py:153
  283.9 0.1 fusion.44
  284.0 0.0 copy-start.7
  284.0 1.1 copy.54
  285.1 1.8 convert_element_type.76
  286.9 6.1 %all-to-all-start.2 = ((bf16[16,6,768]{2,1,0:T(8,128)(2,1)}), bf16[16,6,768]{2,1,0:T(8,128)(2,1)S(1)}, u32[]{:S(2)}, u32[]{:S(2)}) async-start(bf16[16,6,768]{2,1,0:T(8,128)(2,1)} %convert_element_type.76), calls=%async_computation.2 | async-start | bytes 393216 | tf_op jit(solution)/shard_map/all_to_all | solution.py:158
  292.9 0.1 mul.230
  293.0 14.6 %all-to-all-done.2 = bf16[16,6,768]{2,1,0:T(8,128)(2,1)S(1)} async-done(((bf16[16,6,768]{2,1,0:T(8,128)(2,1)}), bf16[16,6,768]{2,1,0:T(8,128)(2,1)S(1)}, u32[]{:S(2)}, u32[]{:S(2)}) %all-to-all-start.2) | async-done | bytes 147488 | tf_op jit(solution)/shard_map/all_to_all | solution.py:158
  307.7 0.7 gather_fusion
  308.4 0.7 fusion.43
  (31 shorter events, 0.3 us)
Async XLA Ops:
  7.2 116.4 %copy-start = (bf16[256,4096]{1,0:T(8,128)(2,1)S(1)}, bf16[256,4096]{1,0:T(8,128)(2,1)}, u32[]{:S(2)}) copy-start(bf16[256,4096]{1,0:T(8,128)(2,1)} %param.17) | copy-start | bytes 6291460
  7.2 25.2 %copy-start.5 = (bf16[128,256]{1,0:T(8,128)(2,1)S(1)}, bf16[128,256]{1,0:T(8,128)(2,1)}, u32[]{:S(2)}) copy-start(bf16[128,256]{1,0:T(8,128)(2,1)} %param.15) | copy-start | bytes 196612
  7.2 25.2 %copy-start.6 = (bf16[128,256]{1,0:T(8,128)(2,1)S(1)}, bf16[128,256]{1,0:T(8,128)(2,1)}, u32[]{:S(2)}) copy-start(bf16[128,256]{1,0:T(8,128)(2,1)} %param.14) | copy-start | bytes 196612
  7.2 270.2 %all-gather.2.cloned.1.call-start = ((), (), s32[]{:S(2)}) async-start(), calls=%async_computation.3 | async-start | bytes 13369344 | tf_op jit(solution)/shard_map/all_gather | solution.py:74
  8.4 65.8 %copy-start.8 = (s32[64]{0:T(128)S(1)}, s32[64]{0:T(128)}, u32[]{:S(2)}) copy-start(s32[64]{0:T(128)} %param.16) | copy-start | bytes 772
  8.5 65.9 %copy-start.9 = (s32[32]{0:T(128)S(1)}, s32[32]{0:T(128)}, u32[]{:S(2)}) copy-start(s32[32]{0:T(128)} %constant.180) | copy-start | bytes 388
  32.4 21.5 %collective-permute-start = (bf16[128,256]{1,0:T(8,128)(2,1)S(1)}, bf16[128,256]{1,0:T(8,128)(2,1)S(1)}, u32[]{:S(2)}, u32[]{:S(2)}) collective-permute-start(bf16[128,256]{1,0:T(8,128)(2,1)S(1)} %pad_maximum_fusion.1), channel_id=1, source_target_pairs={{0,256},{16,272},{32,288},{48,304},{64,320},{80,336},{96,352},{112... | collective-permute-start | bytes 196616 | tf_op jit(solution)/shard_map/ppermute | solution.py:42
  54.0 7.8 %collective-permute-start.1 = (bf16[256,256]{1,0:T(8,128)(2,1)S(1)}, bf16[256,256]{1,0:T(8,128)(2,1)S(1)}, u32[]{:S(2)}, u32[]{:S(2)}) collective-permute-start(bf16[256,256]{1,0:T(8,128)(2,1)S(1)} %maximum_select_fusion.4), channel_id=1, source_target_pairs={{0,128},{16,144},{32,160},{48,176},{64,192},{80,208},{96,224},{112... | collective-permute-start | bytes 393224 | tf_op jit(solution)/shard_map/ppermute | solution.py:42
  61.9 8.2 %collective-permute-start.2 = (bf16[512,256]{1,0:T(8,128)(2,1)S(1)}, bf16[512,256]{1,0:T(8,128)(2,1)S(1)}, u32[]{:S(2)}, u32[]{:S(2)}) collective-permute-start(bf16[512,256]{1,0:T(8,128)(2,1)S(1)} %maximum_select_fusion.3), channel_id=1, source_target_pairs={{0,64},{16,80},{32,96},{48,112},{64,0},{80,16},{96,32},{112,48},{1... | collective-permute-start | bytes 786440 | tf_op jit(solution)/shard_map/ppermute | solution.py:42
  70.3 25.3 %collective-permute-start.3 = (bf16[1024,256]{1,0:T(8,128)(2,1)S(1)}, bf16[1024,256]{1,0:T(8,128)(2,1)S(1)}, u32[]{:S(2)}, u32[]{:S(2)}) collective-permute-start(bf16[1024,256]{1,0:T(8,128)(2,1)S(1)} %maximum_select_fusion.2), channel_id=1, source_target_pairs={{0,32},{16,48},{32,0},{48,16},{64,96},{80,112},{96,64},{112,80},{1... | collective-permute-start | bytes 1572872 | tf_op jit(solution)/shard_map/ppermute | solution.py:42
  95.8 23.5 %collective-permute-start.4 = (bf16[2048,256]{1,0:T(8,128)(2,1)S(1)}, bf16[2048,256]{1,0:T(8,128)(2,1)S(1)}, u32[]{:S(2)}, u32[]{:S(2)}) collective-permute-start(bf16[2048,256]{1,0:T(8,128)(2,1)S(1)} %maximum_select_fusion.1), channel_id=1, source_target_pairs={{0,16},{16,0},{32,48},{48,32},{64,80},{80,64},{96,112},{112,96},{1... | collective-permute-start | bytes 3145736 | tf_op jit(solution)/shard_map/ppermute | solution.py:42
  100.1 19.8 %copy-start.10 = (bf16[128,256]{1,0:T(8,128)(2,1)S(1)}, bf16[128,256]{1,0:T(8,128)(2,1)}, u32[]{:S(2)}) copy-start(bf16[128,256]{1,0:T(8,128)(2,1)} %param.13) | copy-start | bytes 196612
  123.6 44.3 %copy-start.3 = (s32[8,8]{1,0:T(8,128)S(1)}, s32[8,8]{1,0:T(8,128)}, u32[]{:S(2)}) copy-start(s32[8,8]{1,0:T(8,128)} %param.21) | copy-start | bytes 772
  125.1 87.3 %copy-start.2 = (bf16[8,4096]{1,0:T(8,128)(2,1)S(1)}, bf16[8,4096]{1,0:T(8,128)(2,1)}, u32[]{:S(2)}) copy-start(bf16[8,4096]{1,0:T(8,128)(2,1)} %param.12) | copy-start | bytes 196612
  125.1 87.5 %copy-start.4 = (f32[4096]{0:T(1024)S(1)}, f32[4096]{0:T(1024)}, u32[]{:S(2)}) copy-start(f32[4096]{0:T(1024)} %param.18) | copy-start | bytes 49156
  125.1 87.1 %all-to-all-start = ((bf16[16,8,4096]{2,1,0:T(8,128)(2,1)}), bf16[16,8,4096]{2,1,0:T(8,128)(2,1)S(1)}, u32[]{:S(2)}, u32[]{:S(2)}) async-start(bf16[16,8,4096]{2,1,0:T(8,128)(2,1)} %fusion), calls=%async_computation | async-start | bytes 2097152 | tf_op jit(solution)/shard_map/all_to_all | solution.py:129
  212.6 63.4 %copy-start.1 = (bf16[8,4096]{1,0:T(8,128)(2,1)}, bf16[8,4096]{1,0:T(8,128)(2,1)S(1)}, u32[]{:S(2)}) copy-start(bf16[8,4096]{1,0:T(8,128)(2,1)S(1)} %get-tuple-element.9) | copy-start | bytes 196612
  284.0 24.4 %copy-start.7 = (f32[8,8]{1,0:T(8,128)S(1)}, f32[8,8]{1,0:T(8,128)}, u32[]{:S(2)}) copy-start(f32[8,8]{1,0:T(8,128)} %param.22) | copy-start | bytes 772
  286.9 20.7 %all-to-all-start.2 = ((bf16[16,6,768]{2,1,0:T(8,128)(2,1)}), bf16[16,6,768]{2,1,0:T(8,128)(2,1)S(1)}, u32[]{:S(2)}, u32[]{:S(2)}) async-start(bf16[16,6,768]{2,1,0:T(8,128)(2,1)} %convert_element_type.76), calls=%async_computation.2 | async-start | bytes 393216 | tf_op jit(solution)/shard_map/all_to_all | solution.py:158
Sparse Core Ops, SparseCore 0:
  32.4 141.4 all-gather.1
where the time goes:
time: 316 us
  waiting for transfers between devices  129 us (41%)
  blocking collectives  84.5 us (27%)
  starting transfers between devices  62.9 us (20%)
  between operations  14.5 us (5%)
  matrix products  12.1 us (4%)
  local copies, waits for them, and re-layouts  6.76 us (2%)
  other arithmetic  6.11 us (2%)
    ppermute x5, waiting for transfers between devices, gather_by_doubling(): other = lax.ppermute(cur, CTX, [(i, i ^ bit) for i in range(n)])  70.8 us
    all_to_all x1, blocking collectives, shards(): lax.all_to_all(outgoing, EXP, split_axis=0, concat_axis=0, tiled=True)  60.6 us
    all_to_all x1, waiting for transfers between devices, shards(): lax.all_to_all(share.reshape(n_exp, tok_dev, D), EXP, split_axis=0, conca...  43.8 us
    all_to_all x1, starting transfers between devices, shards(): lax.all_to_all(share.reshape(n_exp, tok_dev, D), EXP, split_axis=0, conca...  42.7 us
    all_gather x1, blocking collectives, shards(): w_all = lax.all_gather(w_local, 'zh', axis=0, tiled=True)  23.8 us
    all_to_all x1, waiting for transfers between devices, shards(): lax.all_to_all(hidden.astype(jnp.bfloat16), EXP, split_axis=0, concat_axi...  14.6 us
    ppermute x5, starting transfers between devices, gather_by_doubling(): other = lax.ppermute(cur, CTX, [(i, i ^ bit) for i in range(n)])  14.1 us
    dot_general x1, matrix products, shards(): jnp.einsum('sd,fd->sf', received, w_all, preferred_element_type=jnp.float32)  6.41 us
  transfers between devices with their start and end apart: 8, of which 7 were waited for; matrix products, arithmetic and copies ran while one was open for 4% of the time, Pallas kernels for 0%

commit v1 on v0

--- a/solution.py
+++ b/solution.py
@@ -70,7 +70,8 @@
     n_exp = EXPERTS
     fe_dev = expert_gate.shape[2]
     w_local = jnp.concatenate([expert_gate[0].T, expert_up[0].T], axis=0)
-    w_all = lax.all_gather(w_local, "zh", axis=0, tiled=True)
+    stack = jnp.stack([w_local] * lax.axis_size("zh"))
+    w_all = jnp.concatenate(lax.all_to_all(stack, "zh", 0, 0), axis=0)
     w_all = lax.all_gather(w_all, ("x", "y"), axis=0, tiled=True)
     kv_head = exp_index * per_device // group
     own_keys = lax.dynamic_slice_in_dim(keys, kv_head * HD, HD, 1)

time: 316 us -> 330 us (1.044)
  the two profiles are of different devices: /device:TPU:269 before, /device:TPU:29 now
where the time goes in v1:
time: 330 us
  waiting for transfers between devices  135 us (41%)
  blocking collectives  98.4 us (30%)
  starting transfers between devices  56.5 us (17%)
  between operations  14.5 us (4%)
  matrix products  12.1 us (4%)
  local copies, waits for them, and re-layouts  6.76 us (2%)
  other arithmetic  6.17 us (2%)
    ppermute x5, waiting for transfers between devices, gather_by_doubling(): other = lax.ppermute(cur, CTX, [(i, i ^ bit) for i in range(n)])  77.1 us
    all_to_all x1, blocking collectives, shards(): lax.all_to_all(outgoing, EXP, split_axis=0, concat_axis=0, tiled=True)  60.6 us
    all_to_all x1, waiting for transfers between devices, shards(): lax.all_to_all(share.reshape(n_exp, tok_dev, D), EXP, split_axis=0, conca...  43.8 us
    all_to_all x1, starting transfers between devices, shards(): lax.all_to_all(share.reshape(n_exp, tok_dev, D), EXP, split_axis=0, conca...  38.6 us
    all_to_all x1, blocking collectives, shards(): w_all = jnp.concatenate(lax.all_to_all(stack, 'zh', 0, 0), axis=0)  37.8 us
    all_to_all x1, waiting for transfers between devices, shards(): lax.all_to_all(hidden.astype(jnp.bfloat16), EXP, split_axis=0, concat_axi...  14.6 us
    ppermute x5, starting transfers between devices, gather_by_doubling(): other = lax.ppermute(cur, CTX, [(i, i ^ bit) for i in range(n)])  11.8 us
  transfers between devices with their start and end apart: 8, of which 7 were waited for; matrix products, arithmetic and copies ran while one was open for 4% of the time, Pallas kernels for 0%

profile of v1, /device:TPU:29, one launch (start us, length us, event | category | flops | bytes accessed | tf_op | source)
XLA Modules:
  0.0 329.9 jit_solution(4438537352775024053)
XLA Ops:
  7.2 0.0 copy-start
  7.2 0.0 all-gather.2.cloned.1.call-start
  7.2 1.2 maximum_bitcast_fusion
  8.4 0.1 pad_maximum_fusion
  8.5 0.0 copy-start.8
  8.5 0.0 copy-start.9
  8.5 37.8 %all_to_all.20 = bf16[2,48,4096]{2,1,0:T(8,128)(2,1)} all-to-all(bf16[2,48,4096]{2,1,0:T(8,128)(2,1)S(1)} %pad_maximum_fusion), channel_id=1, replica_groups=mesh['zh'=2,'x'=4,'y'=4,'zl'=8,'c'=2] {'zh'}, dimensions={0} | all-to-all | bytes 1572864 | tf_op jit(solution)/shard_map/all_to_all | solution.py:74
  46.3 0.0 all-gather.2.cloned.1.call-update
  46.5 2.1 collective-permute-start
  48.5 17.2 %collective-permute-done = bf16[128,256]{1,0:T(8,128)(2,1)S(1)} collective-permute-done((bf16[128,256]{1,0:T(8,128)(2,1)S(1)}, bf16[128,256]{1,0:T(8,128)(2,1)S(1)}, u32[]{:S(2)}, u32[]{:S(2)}) %collective-permute-start) | collective-permute-done | bytes 65568 | tf_op jit(solution)/shard_map/ppermute | solution.py:42
  65.8 2.1 collective-permute-start.1
  67.9 5.5 %collective-permute-done.1 = bf16[256,256]{1,0:T(8,128)(2,1)S(1)} collective-permute-done((bf16[256,256]{1,0:T(8,128)(2,1)S(1)}, bf16[256,256]{1,0:T(8,128)(2,1)S(1)}, u32[]{:S(2)}, u32[]{:S(2)}) %collective-permute-start.1) | collective-permute-done | bytes 131104 | tf_op jit(solution)/shard_map/ppermute | solution.py:42
  73.4 0.1 maximum_select_fusion.3
  73.5 2.8 collective-permute-start.2
  76.4 5.2 %collective-permute-done.2 = bf16[512,256]{1,0:T(8,128)(2,1)S(1)} collective-permute-done((bf16[512,256]{1,0:T(8,128)(2,1)S(1)}, bf16[512,256]{1,0:T(8,128)(2,1)S(1)}, u32[]{:S(2)}, u32[]{:S(2)}) %collective-permute-start.2) | collective-permute-done | bytes 262176 | tf_op jit(solution)/shard_map/ppermute | solution.py:42
  81.6 0.2 maximum_select_fusion.2
  81.8 2.9 collective-permute-start.3
  84.7 0.1 select_reduce_fusion.9
  84.8 0.1 iota_add_fusion
  84.9 21.5 %collective-permute-done.3 = bf16[1024,256]{1,0:T(8,128)(2,1)S(1)} collective-permute-done((bf16[1024,256]{1,0:T(8,128)(2,1)S(1)}, bf16[1024,256]{1,0:T(8,128)(2,1)S(1)}, u32[]{:S(2)}, u32[]{:S(2)}) %collective-permute-start.3) | collective-permute-done | bytes 524320 | tf_op jit(solution)/shard_map/ppermute | solution.py:42
  106.4 0.2 maximum_select_fusion.1
  106.6 1.9 collective-permute-start.4
  108.6 0.2 select_reduce_fusion.4
  108.9 0.8 broadcast_compare_fusion.1
  109.7 0.0 copy-start.10
  109.7 27.6 %collective-permute-done.4 = bf16[2048,256]{1,0:T(8,128)(2,1)S(1)} collective-permute-done((bf16[2048,256]{1,0:T(8,128)(2,1)S(1)}, bf16[2048,256]{1,0:T(8,128)(2,1)S(1)}, u32[]{:S(2)}, u32[]{:S(2)}) %collective-permute-start.4) | collective-permute-done | bytes 1048608 | tf_op jit(solution)/shard_map/ppermute | solution.py:42
  137.3 0.5 maximum_select_fusion
  137.9 0.3 select_reduce_fusion
  138.2 0.3 select_reduce_fusion.1
  138.6 0.3 select_reduce_fusion.2
  138.9 0.3 select_reduce_fusion.3
  139.3 0.4 fusion.14
  139.7 0.4 fusion.18
  140.2 0.4 fusion.12
  140.5 0.4 fusion.10
  140.9 0.4 fusion.8
  141.3 0.4 fusion.13
  141.6 0.0 copy-start.3
  141.7 1.5 fusion
  143.2 38.6 %all-to-all-start = ((bf16[16,8,4096]{2,1,0:T(8,128)(2,1)}), bf16[16,8,4096]{2,1,0:T(8,128)(2,1)S(1)}, u32[]{:S(2)}, u32[]{:S(2)}) async-start(bf16[16,8,4096]{2,1,0:T(8,128)(2,1)} %fusion), calls=%async_computation | async-start | bytes 2097152 | tf_op jit(solution)/shard_map/all_to_all | solution.py:130
  181.8 0.1 reshape.363
  181.9 0.1 fusion.59
  182.0 0.1 reduce_window_sum.11
  182.1 0.2 select_reduce_fusion.8
  182.3 0.1 reduce_sum.147
  182.4 0.1 fusion.61
  182.5 43.8 %all-to-all-done = bf16[16,8,4096]{2,1,0:T(8,128)(2,1)S(1)} async-done(((bf16[16,8,4096]{2,1,0:T(8,128)(2,1)}), bf16[16,8,4096]{2,1,0:T(8,128)(2,1)S(1)}, u32[]{:S(2)}, u32[]{:S(2)}) %all-to-all-start) | async-done | bytes 1048608 | tf_op jit(solution)/shard_map/all_to_all | solution.py:130
  226.3 0.1 convert_reduce_fusion
  226.4 0.1 fusion.45
  226.6 1.3 convolution_convert_fusion.1
  227.9 1.4 reshape.364
  229.3 60.6 %all_to_all.21 = bf16[16,6,4096]{2,1,0:T(8,128)(2,1)} all-to-all(bf16[16,6,4096]{2,1,0:T(8,128)(2,1)S(1)} %reshape.364), channel_id=1, replica_groups=mesh['zh'=2,'x'=4,'y'=4,'zl'=8,'c'=2] {'zl','c'}, dimensions={0} | all-to-all | bytes 1572864 | tf_op jit(solution)/shard_map/all_to_all | solution.py:152
  289.9 1.4 reshape.387
  291.4 0.0 all-gather.2.cloned.1.call-done
  291.4 6.4 %fusion.22 = f32[96,16,2,2,24]{0,4,3,2,1:T(8,128)S(1)} fusion(bf16[16,2,2,24,4096]{4,3,2,1,0:T(8,128)(2,1)} %bitcast.297, bf16[96,4096,1,1,1]{1,0,2,3,4:T(8,128)(2,1)S(1)} %reshape.387), kind=kOutput, calls=%fused_computation.45 | convolution fusion | flops 1207959552 | bytes 13959168 | tf_op jit(solution)/shard_map/sd,fd->sf/dot_general | solution.py:154
  297.8 0.1 fusion.44
  298.0 0.0 copy-start.7
  298.0 1.1 copy.54
  299.1 1.8 convert_element_type.76
  300.9 6.1 %all-to-all-start.3 = ((bf16[16,6,768]{2,1,0:T(8,128)(2,1)}), bf16[16,6,768]{2,1,0:T(8,128)(2,1)S(1)}, u32[]{:S(2)}, u32[]{:S(2)}) async-start(bf16[16,6,768]{2,1,0:T(8,128)(2,1)} %convert_element_type.76), calls=%async_computation.3 | async-start | bytes 393216 | tf_op jit(solution)/shard_map/all_to_all | solution.py:159
  306.9 0.1 mul.230
  307.0 14.6 %all-to-all-done.3 = bf16[16,6,768]{2,1,0:T(8,128)(2,1)S(1)} async-done(((bf16[16,6,768]{2,1,0:T(8,128)(2,1)}), bf16[16,6,768]{2,1,0:T(8,128)(2,1)S(1)}, u32[]{:S(2)}, u32[]{:S(2)}) %all-to-all-start.3) | async-done | bytes 147488 | tf_op jit(solution)/shard_map/all_to_all | solution.py:159
  321.6 0.7 gather_fusion
  322.3 0.7 fusion.43
  (32 shorter events, 0.3 us)
Async XLA Ops:
  7.2 134.5 %copy-start = (bf16[256,4096]{1,0:T(8,128)(2,1)S(1)}, bf16[256,4096]{1,0:T(8,128)(2,1)}, u32[]{:S(2)}) copy-start(bf16[256,4096]{1,0:T(8,128)(2,1)} %param.17) | copy-start | bytes 6291460
  7.2 284.2 %all-gather.2.cloned.1.call-start = ((), (), s32[]{:S(2)}) async-start(), calls=%async_computation.4 | async-start | bytes 13369344 | tf_op jit(solution)/shard_map/all_gather | solution.py:75
  7.2 39.2 %copy-start.5 = (bf16[128,256]{1,0:T(8,128)(2,1)S(1)}, bf16[128,256]{1,0:T(8,128)(2,1)}, u32[]{:S(2)}) copy-start(bf16[128,256]{1,0:T(8,128)(2,1)} %param.15) | copy-start | bytes 196612
  7.2 39.2 %copy-start.6 = (bf16[128,256]{1,0:T(8,128)(2,1)S(1)}, bf16[128,256]{1,0:T(8,128)(2,1)}, u32[]{:S(2)}) copy-start(bf16[128,256]{1,0:T(8,128)(2,1)} %param.14) | copy-start | bytes 196612
  8.5 76.2 %copy-start.8 = (s32[64]{0:T(128)S(1)}, s32[64]{0:T(128)}, u32[]{:S(2)}) copy-start(s32[64]{0:T(128)} %param.16) | copy-start | bytes 772
  8.5 76.3 %copy-start.9 = (s32[32]{0:T(128)S(1)}, s32[32]{0:T(128)}, u32[]{:S(2)}) copy-start(s32[32]{0:T(128)} %constant.180) | copy-start | bytes 388
  46.5 19.3 %collective-permute-start = (bf16[128,256]{1,0:T(8,128)(2,1)S(1)}, bf16[128,256]{1,0:T(8,128)(2,1)S(1)}, u32[]{:S(2)}, u32[]{:S(2)}) collective-permute-start(bf16[128,256]{1,0:T(8,128)(2,1)S(1)} %pad_maximum_fusion.1), channel_id=1, source_target_pairs={{0,256},{16,272},{32,288},{48,304},{64,320},{80,336},{96,352},{112... | collective-permute-start | bytes 196616 | tf_op jit(solution)/shard_map/ppermute | solution.py:42
  65.8 7.7 %collective-permute-start.1 = (bf16[256,256]{1,0:T(8,128)(2,1)S(1)}, bf16[256,256]{1,0:T(8,128)(2,1)S(1)}, u32[]{:S(2)}, u32[]{:S(2)}) collective-permute-start(bf16[256,256]{1,0:T(8,128)(2,1)S(1)} %maximum_select_fusion.4), channel_id=1, source_target_pairs={{0,128},{16,144},{32,160},{48,176},{64,192},{80,208},{96,224},{112... | collective-permute-start | bytes 393224 | tf_op jit(solution)/shard_map/ppermute | solution.py:42
  73.5 8.0 %collective-permute-start.2 = (bf16[512,256]{1,0:T(8,128)(2,1)S(1)}, bf16[512,256]{1,0:T(8,128)(2,1)S(1)}, u32[]{:S(2)}, u32[]{:S(2)}) collective-permute-start(bf16[512,256]{1,0:T(8,128)(2,1)S(1)} %maximum_select_fusion.3), channel_id=1, source_target_pairs={{0,64},{16,80},{32,96},{48,112},{64,0},{80,16},{96,32},{112,48},{1... | collective-permute-start | bytes 786440 | tf_op jit(solution)/shard_map/ppermute | solution.py:42
  81.8 24.6 %collective-permute-start.3 = (bf16[1024,256]{1,0:T(8,128)(2,1)S(1)}, bf16[1024,256]{1,0:T(8,128)(2,1)S(1)}, u32[]{:S(2)}, u32[]{:S(2)}) collective-permute-start(bf16[1024,256]{1,0:T(8,128)(2,1)S(1)} %maximum_select_fusion.2), channel_id=1, source_target_pairs={{0,32},{16,48},{32,0},{48,16},{64,96},{80,112},{96,64},{112,80},{1... | collective-permute-start | bytes 1572872 | tf_op jit(solution)/shard_map/ppermute | solution.py:42
  106.6 30.7 %collective-permute-start.4 = (bf16[2048,256]{1,0:T(8,128)(2,1)S(1)}, bf16[2048,256]{1,0:T(8,128)(2,1)S(1)}, u32[]{:S(2)}, u32[]{:S(2)}) collective-permute-start(bf16[2048,256]{1,0:T(8,128)(2,1)S(1)} %maximum_select_fusion.1), channel_id=1, source_target_pairs={{0,16},{16,0},{32,48},{48,32},{64,80},{80,64},{96,112},{112,96},{1... | collective-permute-start | bytes 3145736 | tf_op jit(solution)/shard_map/ppermute | solution.py:42
  109.7 28.2 %copy-start.10 = (bf16[128,256]{1,0:T(8,128)(2,1)S(1)}, bf16[128,256]{1,0:T(8,128)(2,1)}, u32[]{:S(2)}) copy-start(bf16[128,256]{1,0:T(8,128)(2,1)} %param.13) | copy-start | bytes 196612
  141.6 40.2 %copy-start.3 = (s32[8,8]{1,0:T(8,128)S(1)}, s32[8,8]{1,0:T(8,128)}, u32[]{:S(2)}) copy-start(s32[8,8]{1,0:T(8,128)} %param.21) | copy-start | bytes 772
  143.2 83.2 %copy-start.2 = (bf16[8,4096]{1,0:T(8,128)(2,1)S(1)}, bf16[8,4096]{1,0:T(8,128)(2,1)}, u32[]{:S(2)}) copy-start(bf16[8,4096]{1,0:T(8,128)(2,1)} %param.12) | copy-start | bytes 196612
  143.2 83.4 %copy-start.4 = (f32[4096]{0:T(1024)S(1)}, f32[4096]{0:T(1024)}, u32[]{:S(2)}) copy-start(f32[4096]{0:T(1024)} %param.18) | copy-start | bytes 49156
  143.2 83.1 %all-to-all-start = ((bf16[16,8,4096]{2,1,0:T(8,128)(2,1)}), bf16[16,8,4096]{2,1,0:T(8,128)(2,1)S(1)}, u32[]{:S(2)}, u32[]{:S(2)}) async-start(bf16[16,8,4096]{2,1,0:T(8,128)(2,1)} %fusion), calls=%async_computation | async-start | bytes 2097152 | tf_op jit(solution)/shard_map/all_to_all | solution.py:130
  226.6 63.4 %copy-start.1 = (bf16[8,4096]{1,0:T(8,128)(2,1)}, bf16[8,4096]{1,0:T(8,128)(2,1)S(1)}, u32[]{:S(2)}) copy-start(bf16[8,4096]{1,0:T(8,128)(2,1)S(1)} %get-tuple-element.9) | copy-start | bytes 196612
  298.0 24.4 %copy-start.7 = (f32[8,8]{1,0:T(8,128)S(1)}, f32[8,8]{1,0:T(8,128)}, u32[]{:S(2)}) copy-start(f32[8,8]{1,0:T(8,128)} %param.22) | copy-start | bytes 772
  300.9 20.7 %all-to-all-start.3 = ((bf16[16,6,768]{2,1,0:T(8,128)(2,1)}), bf16[16,6,768]{2,1,0:T(8,128)(2,1)S(1)}, u32[]{:S(2)}, u32[]{:S(2)}) async-start(bf16[16,6,768]{2,1,0:T(8,128)(2,1)} %convert_element_type.76), calls=%async_computation.3 | async-start | bytes 393216 | tf_op jit(solution)/shard_map/all_to_all | solution.py:159
Sparse Core Ops, SparseCore 0:
  46.5 138.1 all-gather.1
